TPU v7x, 512 devices: a whole 4x8x8 slice. The times are simulated.
512 devices in a mesh: section: 32 (over y, z_lo, core), tensor: 16 (over x, z_hi).
Axes of the slice: x: 4, y: 8, z: 8 (z_hi: 4, z_lo: 2; z = z_hi * 2 + z_lo), core: 2. Of those that a mesh axis runs over, the one named last changes fastest.
Arguments:
- tokens: bfloat16 [768, 8192], P('section', 'tensor'), may hold values from -6 to 6
- out_grad: bfloat16 [768, 8192], P('section', 'tensor'), may hold values from -3 to 3
- gate_weight: bfloat16 [8192, 14336], P('tensor', 'section'), may hold values from -0.0625 to 0.0625
- up_weight: bfloat16 [8192, 14336], P('tensor', 'section'), may hold values from -0.0625 to 0.0625
- down_weight: bfloat16 [14336, 8192], P('section', 'tensor'), may hold values from -0.046875 to 0.046875
Outputs:
- grad_input: bfloat16 [768, 8192], P('section', 'tensor')
- grad_gate: bfloat16 [8192, 14336], P('tensor', 'section')
- grad_up: bfloat16 [8192, 14336], P('tensor', 'section')
- grad_down: bfloat16 [14336, 8192], P('section', 'tensor')
All inputs are finite; a program needn't handle non-finite values.
Results may differ from a plain program's by a relative error of at most 0.0049.
Values may be sent and summed in bfloat16 or wider, within the bound.
No kernel may reach another device: no remote copies, remote signals or barrier semaphores. Data moves between devices by JAX's collectives and lax.ppermute only.
A program may use at most 64 MiB of HBM per device.

v0:
```python
import jax
import jax.numpy as jnp
from jax import lax
from jax.sharding import Mesh, PartitionSpec as P


def swiglu_grads(gate_value, up_value, hidden_grad):
    logistic = jax.nn.sigmoid(gate_value)
    swish = gate_value * logistic
    hidden = (swish * up_value).astype(jnp.bfloat16)
    up_delta = (hidden_grad * swish).astype(jnp.bfloat16)
    gate_delta = (hidden_grad * up_value * logistic * (1.0 + gate_value * (1.0 - logistic))).astype(
        jnp.bfloat16
    )
    return (hidden, gate_delta, up_delta)


SEC = ("y", "zl", "c")
TEN = ("x", "zh")


def scatter_sum(v, axis_name, n, dim):
    shape = v.shape
    v = v.reshape(shape[:dim] + (n, shape[dim] // n) + shape[dim + 1 :])
    v = lax.all_to_all(v, axis_name, dim, dim, tiled=True)
    return v.sum(dim)


def local(tokens, out_grad, gate_weight, up_weight, down_weight, nx, nzh, nsec):
    contract_last = (((1,), (1,)), ((), ()))
    contract_first = (((0,), (0,)), ((), ()))
    all_tokens, all_grads = (
        lax.all_gather(tokens, SEC, axis=0, tiled=True),
        lax.all_gather(out_grad, SEC, axis=0, tiled=True),
    )
    gate_part = jnp.dot(all_tokens, gate_weight, preferred_element_type=jnp.float32)
    up_part = jnp.dot(all_tokens, up_weight, preferred_element_type=jnp.float32)
    hidden_part = lax.dot_general(
        all_grads, down_weight, contract_last, preferred_element_type=jnp.float32
    )
    parts = jnp.stack([gate_part, up_part, hidden_part])
    parts = scatter_sum(parts, "x", nx, 1)
    parts = scatter_sum(parts, "zh", nzh, 1)
    hidden, gate_delta, up_delta = swiglu_grads(parts[0], parts[1], parts[2])
    deltas = lax.all_gather(jnp.stack([hidden, gate_delta, up_delta]), TEN, axis=1, tiled=True)
    hidden, gate_delta, up_delta = (deltas[0], deltas[1], deltas[2])
    grad_down = lax.dot_general(
        hidden, all_grads, contract_first, preferred_element_type=jnp.float32
    ).astype(jnp.bfloat16)
    grad_gate = lax.dot_general(
        all_tokens, gate_delta, contract_first, preferred_element_type=jnp.float32
    ).astype(jnp.bfloat16)
    grad_up = lax.dot_general(
        all_tokens, up_delta, contract_first, preferred_element_type=jnp.float32
    ).astype(jnp.bfloat16)
    result = lax.dot_general(
        gate_delta, gate_weight, contract_last, preferred_element_type=jnp.float32
    ) + lax.dot_general(up_delta, up_weight, contract_last, preferred_element_type=jnp.float32)
    grad_input = scatter_sum(result, SEC, nsec, 0).astype(jnp.bfloat16)
    return (grad_input, grad_gate, grad_up, grad_down)


def solution(mesh):
    nsec, nten = (mesh.shape["section"], mesh.shape["tensor"])
    nzh = 4
    nx = nten // nzh
    fine = Mesh(mesh.devices.reshape(nsec // 4, 2, 2, nx, nzh), ("y", "zl", "c", "x", "zh"))
    act = P(SEC, TEN)
    wt = P(TEN, SEC)

    def body(*args):
        return local(*args, nx=nx, nzh=nzh, nsec=nsec)

    return jax.shard_map(
        body,
        mesh=fine,
        in_specs=(act, act, wt, wt, act),
        out_specs=(act, wt, wt, act),
        check_vma=False,
    )
```

profile of v0, /device:TPU:1, one launch (start us, length us, event | category | flops | bytes accessed | tf_op | source)
XLA Modules:
  0.0 305.4 jit_solution(14879705945797379860)
XLA Ops:
  7.2 0.0 copy-start
  7.2 0.0 all-gather.2.cloned.1.call-start
  7.2 39.7 %all_gather.9 = bf16[768,512]{1,0:T(8,128)(2,1)S(1)} all-gather(bf16[24,512]{1,0:T(8,128)(2,1)} %param.5), channel_id=1, replica_groups=mesh['y'=8,'zl'=2,'c'=2,'x'=4,'zh'=4] {'y','zl','c'}, dimensions={0}, use_global_device_ids=true | all-gather | bytes 811008 | tf_op jit(solution)/shard_map/all_gather | solution.py:33
  46.9 34.7 %all_gather.10 = bf16[768,512]{1,0:T(8,128)(2,1)S(1)} all-gather(bf16[24,512]{1,0:T(8,128)(2,1)} %param.6), channel_id=1, replica_groups=mesh['y'=8,'zl'=2,'c'=2,'x'=4,'zh'=4] {'y','zl','c'}, dimensions={0}, use_global_device_ids=true | all-gather | bytes 811008 | tf_op jit(solution)/shard_map/all_gather | solution.py:34
  81.6 0.0 copy-start.1
  81.6 0.0 copy-start.4
  81.6 1.9 fusion.5
  83.5 0.0 copy-done
  83.5 0.6 fusion.4
  84.1 0.0 copy-done.1
  84.1 0.0 copy-done.4
  84.1 0.6 fusion.6
  84.7 0.5 pad_maximum_fusion
  85.3 0.5 copy.19
  85.8 57.6 %all_to_all.15 = f32[3,4,192,448]{3,2,0,1:T(8,128)} all-to-all(f32[3,4,192,448]{3,2,0,1:T(8,128)S(1)} %copy.19), channel_id=1, replica_groups=mesh['y'=8,'zl'=2,'c'=2,'x'=4,'zh'=4] {'x'}, dimensions={1} | all-to-all | bytes 8257536 | tf_op jit(solution)/shard_map/all_to_all | solution.py:25
  143.4 3.1 %reduce_sum.27 = f32[3,192,448]{2,1,0:T(8,128)S(1)} reduce(f32[3,4,192,448]{3,2,0,1:T(8,128)} %all_to_all.15, f32[]{:T(128)} %constant.0.clone.1), dimensions={1}, to_apply=%region_0.0 | reduce | flops 774144 | bytes 5160964 | tf_op jit(solution)/shard_map/reduce_sum | solution.py:26
  146.4 0.1 copy.20
  146.6 30.6 %all_to_all.16 = f32[3,4,48,448]{3,2,0,1:T(8,128)S(1)} all-to-all(f32[3,4,48,448]{3,2,0,1:T(8,128)S(1)} %copy.20), channel_id=1, replica_groups=mesh['y'=8,'zl'=2,'c'=2,'x'=4,'zh'=4] {'zh'}, dimensions={1} | all-to-all | bytes 2064384 | tf_op jit(solution)/shard_map/all_to_all | solution.py:25
  177.2 0.0 copy-start.2
  177.2 0.1 reduce_sum.28
  177.3 0.1 multiply_convert_fusion.2
  177.4 0.7 pad_maximum_fusion.1
  178.1 0.0 all-gather.2.cloned.1.call-update
  178.1 67.0 %all-gather.2.cloned.1.call-done = bf16[3,768,448]{2,1,0:T(8,128)(2,1)} async-done(((bf16[3,48,448]{2,1,0:T(8,128)(2,1)}), bf16[3,768,448]{2,1,0:T(8,128)(2,1)}) %all-gather.2.cloned.1.call-update) | async-done | bytes 2064400 | tf_op jit(solution)/shard_map/all_gather | solution.py:45
  245.1 1.7 fusion.2
  246.8 0.0 copy-done.2
  246.8 2.8 convolution_add_fusion
  249.6 9.0 %all-to-all-start.2 = ((f32[32,24,512]{2,1,0:T(8,128)}), f32[32,24,512]{2,1,0:T(8,128)S(1)}, u32[]{:S(2)}, u32[]{:S(2)}) async-start(f32[32,24,512]{2,1,0:T(8,128)} %bitcast.31), calls=%async_computation.2 | async-start | bytes 3145728 | tf_op jit(solution)/shard_map/all_to_all | solution.py:25
  258.7 0.0 copy-start.3
  258.7 2.8 convolution_convert_fusion
  261.5 0.0 copy-done.3
  261.5 1.3 fusion.1
  262.8 1.3 fusion
  264.2 33.7 %all-to-all-done.2 = f32[32,24,512]{2,1,0:T(8,128)S(1)} async-done(((f32[32,24,512]{2,1,0:T(8,128)}), f32[32,24,512]{2,1,0:T(8,128)S(1)}, u32[]{:S(2)}, u32[]{:S(2)}) %all-to-all-start.2) | async-done | bytes 1572896 | tf_op jit(solution)/shard_map/all_to_all | solution.py:25
  297.9 0.7 reduce_sum.29
Async XLA Ops:
  7.2 76.3 %copy-start = (bf16[512,448]{0,1:T(8,128)(2,1)S(1)}, bf16[512,448]{0,1:T(8,128)(2,1)}, u32[]{:S(2)}) copy-start(bf16[512,448]{0,1:T(8,128)(2,1)} %param.7) | copy-start | bytes 1376260
  7.2 237.9 %all-gather.2.cloned.1.call-start = ((), (), s32[]{:S(2)}) async-start(), calls=%async_computation.3 | async-start | bytes 2506752 | tf_op jit(solution)/shard_map/all_gather | solution.py:45
  81.6 2.5 copy-start.1
  81.6 2.5 copy-start.4
  177.2 69.6 %copy-start.2 = (bf16[512,448]{0,1:T(8,128)(2,1)S(1)}, bf16[512,448]{0,1:T(8,128)(2,1)}, u32[]{:S(2)}) copy-start(bf16[512,448]{0,1:T(8,128)(2,1)} %param.8) | copy-start | bytes 1376260
  249.6 48.2 %all-to-all-start.2 = ((f32[32,24,512]{2,1,0:T(8,128)}), f32[32,24,512]{2,1,0:T(8,128)S(1)}, u32[]{:S(2)}, u32[]{:S(2)}) async-start(f32[32,24,512]{2,1,0:T(8,128)} %bitcast.31), calls=%async_computation.2 | async-start | bytes 3145728 | tf_op jit(solution)/shard_map/all_to_all | solution.py:25
  258.7 2.9 copy-start.3
Sparse Core Ops, SparseCore 0:
  178.2 66.8 all-gather.1
where the time goes:
time: 306 us; the launch traced here: 305 us
  blocking collectives  163 us (53%)
  waiting for transfers between devices  101 us (33%)
  between operations  14.1 us (5%)
  matrix products  13.1 us (4%)
  starting transfers between devices  9.06 us (3%)
  other arithmetic  5.16 us (2%)
    all_to_all x2, blocking collectives, scatter_sum(): v = lax.all_to_all(v, axis_name, dim, dim, tiled=True)  88.2 us
    all_gather x1, waiting for transfers between devices, local(): lax.all_gather(jnp.stack([hidden, gate_delta, up_delta]), TEN, axis=1, ti...  67 us
    all_gather x1, blocking collectives, local(): lax.all_gather(tokens, SEC, axis=0, tiled=True)  39.7 us
    all_gather x1, blocking collectives, local(): lax.all_gather(out_grad, SEC, axis=0, tiled=True)  34.7 us
    all_to_all x1, waiting for transfers between devices, scatter_sum(): v = lax.all_to_all(v, axis_name, dim, dim, tiled=True)  33.7 us
    all_to_all x1, starting transfers between devices, scatter_sum(): v = lax.all_to_all(v, axis_name, dim, dim, tiled=True)  9.03 us
  transfers between devices with their start and end apart: 2, of which 2 were waited for; matrix products, arithmetic and copies ran while one was open for 2% of the time, Pallas kernels for 0%

commit v1 on v0

--- a/solution.py
+++ b/solution.py
@@ -2,6 +2,7 @@
 import jax.numpy as jnp
 from jax import lax
 from jax.sharding import Mesh, PartitionSpec as P
+from jax.lax import all_to_all, axis_size
 
 
 def swiglu_grads(gate_value, up_value, hidden_grad):
@@ -29,9 +30,16 @@
 def local(tokens, out_grad, gate_weight, up_weight, down_weight, nx, nzh, nsec):
     contract_last = (((1,), (1,)), ((), ()))
     contract_first = (((0,), (0,)), ((), ()))
+
+    def _search_waves(mat, peer_axis):
+        inter = axis_size(peer_axis)
+        near = jnp.stack(inter * [mat])
+        carry_in = all_to_all(near, peer_axis, 0, 0)
+        return jnp.concatenate(carry_in, axis=0)
+
     all_tokens, all_grads = (
         lax.all_gather(tokens, SEC, axis=0, tiled=True),
-        lax.all_gather(out_grad, SEC, axis=0, tiled=True),
+        _search_waves(out_grad, SEC),
     )
     gate_part = jnp.dot(all_tokens, gate_weight, preferred_element_type=jnp.float32)
     up_part = jnp.dot(all_tokens, up_weight, preferred_element_type=jnp.float32)

time: 306 us -> 297 us (0.971)
  blocking collectives: 163 us -> 137 us
  starting transfers between devices: 9.06 us -> 20.2 us
    all_gather x1 -> x0, blocking collectives: 34.7 us -> none  [local(): lax.all_gather(out_grad, SEC, axis=0, tiled=True)]
    all_to_all x0 -> x1, starting transfers between devices: none -> 11.1 us  [_search_waves(): carry_in = all_to_all(near, peer_axis, 0, 0)]
    all_gather x1, blocking collectives: 39.7 us -> 47.7 us  [local(): lax.all_gather(tokens, SEC, axis=0, tiled=True)]
  transfers between devices with their start and end apart: 2 -> 3, of which waited for: 2 -> 2; matrix products, arithmetic and copies ran while one was open for 2% -> 3% of each run, Pallas kernels for 0% -> 0%
where the time goes in v1:
time: 297 us
  blocking collectives  137 us (46%)
  waiting for transfers between devices  102 us (34%)
  starting transfers between devices  20.2 us (7%)
  matrix products  15.2 us (5%)
  between operations  14.2 us (5%)
  other arithmetic  5.31 us (2%)
    all_to_all x2, blocking collectives, scatter_sum(): v = lax.all_to_all(v, axis_name, dim, dim, tiled=True)  89.6 us
    all_gather x1, waiting for transfers between devices, local(): lax.all_gather(jnp.stack([hidden, gate_delta, up_delta]), TEN, axis=1, ti...  69.5 us
    all_gather x1, blocking collectives, local(): lax.all_gather(tokens, SEC, axis=0, tiled=True)  47.7 us
    all_to_all x1, waiting for transfers between devices, scatter_sum(): v = lax.all_to_all(v, axis_name, dim, dim, tiled=True)  32.8 us
    all_to_all x1, starting transfers between devices, _search_waves(): carry_in = all_to_all(near, peer_axis, 0, 0)  11.1 us
    all_to_all x1, starting transfers between devices, scatter_sum(): v = lax.all_to_all(v, axis_name, dim, dim, tiled=True)  9.03 us
  transfers between devices with their start and end apart: 3, of which 2 were waited for; matrix products, arithmetic and copies ran while one was open for 3% of the time, Pallas kernels for 0%

profile of v1, /device:TPU:1, one launch (start us, length us, event | category | flops | bytes accessed | tf_op | source)
XLA Modules:
  0.0 296.8 jit_solution(13251399545818002337)
XLA Ops:
  7.2 0.0 copy-start
  7.2 0.0 copy-start.4
  7.2 0.0 copy-start.2
  7.2 1.8 stack.12
  9.0 11.1 %all-to-all-start = ((bf16[32,24,512]{2,1,0:T(8,128)(2,1)}), bf16[32,24,512]{2,1,0:T(8,128)(2,1)}, u32[]{:S(2)}, u32[]{:S(2)}) async-start(bf16[32,24,512]{2,1,0:T(8,128)(2,1)} %stack.12), calls=%async_computation | async-start | bytes 1572864 | tf_op jit(solution)/shard_map/all_to_all | solution.py:37
  20.1 0.0 all-gather.2.cloned.1.call-start
  20.1 0.0 copy-done.4
  20.1 47.7 %all_gather.6 = bf16[768,512]{1,0:T(8,128)(2,1)S(1)} all-gather(bf16[24,512]{1,0:T(8,128)(2,1)S(1)} %copy-done.4), channel_id=1, replica_groups=mesh['y'=8,'zl'=2,'c'=2,'x'=4,'zh'=4] {'y','zl','c'}, dimensions={0}, use_global_device_ids=true | all-gather | bytes 811008 | tf_op jit(solution)/shard_map/all_gather | solution.py:41
  67.8 0.0 copy-done.2
  67.8 0.6 fusion.6
  68.4 0.0 copy-done
  68.4 1.8 fusion.5
  70.2 0.0 all-to-all-done
  70.2 0.0 copy-start.1
  70.2 2.0 convolution_bitcast_fusion
  72.1 0.0 copy-done.1
  72.1 0.7 pad_maximum_fusion
  72.8 0.5 copy.18
  73.3 57.6 %all_to_all.20 = f32[3,4,192,448]{3,2,0,1:T(8,128)} all-to-all(f32[3,4,192,448]{3,2,0,1:T(8,128)S(1)} %copy.18), channel_id=1, replica_groups=mesh['y'=8,'zl'=2,'c'=2,'x'=4,'zh'=4] {'x'}, dimensions={1} | all-to-all | bytes 8257536 | tf_op jit(solution)/shard_map/all_to_all | solution.py:26
  130.9 3.1 %reduce_sum.27 = f32[3,192,448]{2,1,0:T(8,128)S(1)} reduce(f32[3,4,192,448]{3,2,0,1:T(8,128)} %all_to_all.20, f32[]{:T(128)} %constant.0.clone.1), dimensions={1}, to_apply=%region_0.0 | reduce | flops 774144 | bytes 5160964 | tf_op jit(solution)/shard_map/reduce_sum | solution.py:27
  134.0 0.1 copy.19
  134.1 31.9 %all_to_all.21 = f32[3,4,48,448]{3,2,0,1:T(8,128)S(1)} all-to-all(f32[3,4,48,448]{3,2,0,1:T(8,128)S(1)} %copy.19), channel_id=1, replica_groups=mesh['y'=8,'zl'=2,'c'=2,'x'=4,'zh'=4] {'zh'}, dimensions={1} | all-to-all | bytes 2064384 | tf_op jit(solution)/shard_map/all_to_all | solution.py:26
  166.1 0.1 reduce_sum.28
  166.2 0.1 multiply_convert_fusion.2
  166.3 0.7 pad_maximum_fusion.1
  167.0 0.0 all-gather.2.cloned.1.call-update
  167.0 69.5 %all-gather.2.cloned.1.call-done = bf16[3,768,448]{2,1,0:T(8,128)(2,1)} async-done(((bf16[3,48,448]{2,1,0:T(8,128)(2,1)}), bf16[3,768,448]{2,1,0:T(8,128)(2,1)}) %all-gather.2.cloned.1.call-update) | async-done | bytes 2064400 | tf_op jit(solution)/shard_map/all_gather | solution.py:53
  236.5 1.7 fusion.2
  238.2 2.8 convolution_add_fusion
  241.1 9.0 %all-to-all-start.3 = ((f32[32,24,512]{2,1,0:T(8,128)}), f32[32,24,512]{2,1,0:T(8,128)S(1)}, u32[]{:S(2)}, u32[]{:S(2)}) async-start(f32[32,24,512]{2,1,0:T(8,128)} %bitcast.36), calls=%async_computation.3 | async-start | bytes 3145728 | tf_op jit(solution)/shard_map/all_to_all | solution.py:26
  250.1 0.0 copy-start.3
  250.1 2.6 fusion.1
  252.7 0.0 copy-done.3
  252.7 1.3 fusion
  254.0 2.4 convolution_convert_fusion
  256.5 32.8 %all-to-all-done.3 = f32[32,24,512]{2,1,0:T(8,128)S(1)} async-done(((f32[32,24,512]{2,1,0:T(8,128)}), f32[32,24,512]{2,1,0:T(8,128)S(1)}, u32[]{:S(2)}, u32[]{:S(2)}) %all-to-all-start.3) | async-done | bytes 1572896 | tf_op jit(solution)/shard_map/all_to_all | solution.py:26
  289.3 0.7 reduce_sum.29
Async XLA Ops:
  7.2 61.2 %copy-start = (bf16[512,448]{0,1:T(8,128)(2,1)S(1)}, bf16[512,448]{0,1:T(8,128)(2,1)}, u32[]{:S(2)}) copy-start(bf16[512,448]{0,1:T(8,128)(2,1)} %param.7) | copy-start | bytes 1376260
  7.2 12.9 %copy-start.4 = (bf16[24,512]{1,0:T(8,128)(2,1)S(1)}, bf16[24,512]{1,0:T(8,128)(2,1)}, u32[]{:S(2)}) copy-start(bf16[24,512]{1,0:T(8,128)(2,1)} %param.5) | copy-start | bytes 73732
  7.2 60.6 %copy-start.2 = (bf16[512,448]{0,1:T(8,128)(2,1)S(1)}, bf16[512,448]{0,1:T(8,128)(2,1)}, u32[]{:S(2)}) copy-start(bf16[512,448]{0,1:T(8,128)(2,1)} %param.8) | copy-start | bytes 1376260
  9.0 61.2 %all-to-all-start = ((bf16[32,24,512]{2,1,0:T(8,128)(2,1)}), bf16[32,24,512]{2,1,0:T(8,128)(2,1)}, u32[]{:S(2)}, u32[]{:S(2)}) async-start(bf16[32,24,512]{2,1,0:T(8,128)(2,1)} %stack.12), calls=%async_computation | async-start | bytes 1572864 | tf_op jit(solution)/shard_map/all_to_all | solution.py:37
  20.1 216.5 %all-gather.2.cloned.1.call-start = ((), (), s32[]{:S(2)}) async-start(), calls=%async_computation.4 | async-start | bytes 2506752 | tf_op jit(solution)/shard_map/all_gather | solution.py:53
  70.2 2.0 copy-start.1
  241.1 48.2 %all-to-all-start.3 = ((f32[32,24,512]{2,1,0:T(8,128)}), f32[32,24,512]{2,1,0:T(8,128)S(1)}, u32[]{:S(2)}, u32[]{:S(2)}) async-start(f32[32,24,512]{2,1,0:T(8,128)} %bitcast.36), calls=%async_computation.3 | async-start | bytes 3145728 | tf_op jit(solution)/shard_map/all_to_all | solution.py:26
  250.1 2.6 copy-start.3
Sparse Core Ops, SparseCore 0:
  167.1 69.3 all-gather.1
